TPU v7x, 256 devices: a whole 4x4x8 slice. The times are simulated.
256 devices in a mesh: section: 4 (over z_lo, core), dp: 64 (over y, x, z_hi).
Axes of the slice: x: 4, y: 4, z: 8 (z_hi: 4, z_lo: 2; z = z_hi * 2 + z_lo), core: 2. Of those that a mesh axis runs over, the one named last changes fastest.
Arguments:
- activations_in: bfloat16 [2, 4096, 8192], P(None, 'dp'), may hold values from -6 to 6
- cotangent: bfloat16 [2, 4096, 8192], P(None, 'dp'), may hold values from -6 to 6
- value_tiles: bfloat16 [4, 128, 128, 128], P('section'), may hold values from -0.0625 to 0.0625
- value_ids: int32 [4, 128], P('section'), may hold values from 0 to 255, as said below
- out_tiles: bfloat16 [4, 192, 128, 128], P('section', 'dp'), may hold values from -0.25 to 0.25
- out_ids: int32 [4, 192], P('section'), may hold values from 0 to 255, as said below
- out_count: int32 [4, 64], P('section'), may hold values from 1 to 3, as said below
Outputs:
- section_outputs: bfloat16 [4, 2, 4096, 8192], P('section', None, 'dp')
- input_grads: bfloat16 [4, 2, 4096, 8192], P('section', None, 'dp')
- out_grad: float32 [4, 192, 128, 128], P('section', 'dp')
Inputs may be any that keep to these rules, and one draw needn't show every extreme that they name: `value_ids`: for each layer, 128 different tile numbers. `out_ids`: for each layer, 192 different tile numbers; slot g lies on index g // 3 of dp. The live slots of an index of dp are its first out_count slots; in each layer some index has all 3 slots live.
All inputs are finite; a program needn't handle non-finite values.
Results may differ from a plain program's by a relative error of at most 0.008.
Values may be sent and summed in bfloat16 or wider, within the bound.
No kernel may reach another device: no remote copies, remote signals or barrier semaphores. Data moves between devices by JAX's collectives and lax.ppermute only.
A program may use at most 192 MiB of HBM per device.

v0:
```python
import math
import jax
import jax.numpy as jnp
from jax import lax
from jax.sharding import PartitionSpec as P

VW = 512


def from_behind(value, axis, steps):
    count = lax.axis_size(axis)
    first, last = (max(0, -steps), min(count, count - steps))
    return lax.ppermute(value, axis, [(source, source + steps) for source in range(first, last)])


def build_blocks(tile_data, tile_ids, row_blocks, col_blocks):
    tile_width = tile_data.shape[-1]
    grid = jnp.zeros((row_blocks * col_blocks, tile_width, tile_width), jnp.bfloat16)
    grid = grid.at[tile_ids].set(tile_data)
    return grid.reshape(row_blocks, col_blocks, tile_width, tile_width)


def on_device(activations_in, cotangent, value_tiles, value_ids, out_tiles, out_ids, out_count):
    section_index = lax.axis_index("section")
    section_count = lax.axis_size("section")
    shard_count = lax.axis_size("dp")
    shard_index = lax.axis_index("dp")
    micro_count = activations_in.shape[0]
    tok_rows = activations_in.shape[1]
    model_width = activations_in.shape[2]
    all_rows = micro_count * tok_rows
    tile_width = value_tiles.shape[-1]
    value_width = VW
    value_blocks = value_width // tile_width
    model_blocks = model_width // tile_width
    slot_share = out_tiles.shape[1]
    out_slot = out_ids[0]
    live_mask = (jnp.arange(slot_share, dtype=jnp.int32)[None, :] < out_count[0][:, None]).reshape(
        -1
    )
    own_live = lax.dynamic_slice_in_dim(live_mask, shard_index * slot_share, slot_share)
    gathered = lax.all_gather(out_tiles[0], "dp", axis=0, tiled=True)
    masked_tiles = jnp.where(live_mask[:, None, None], gathered, jnp.zeros_like(gathered))
    value_grid = build_blocks(value_tiles[0], value_ids[0], model_blocks, value_blocks)
    out_grid = build_blocks(masked_tiles, out_slot, value_blocks, model_blocks)

    def forward_layer(operands):
        hidden, old_values, old_result = operands
        hidden_blocked = hidden.reshape(all_rows, model_blocks, tile_width)
        value_rows = jnp.einsum(
            "rbi,bvij->rvj", hidden_blocked, value_grid, preferred_element_type=jnp.float32
        ).astype(jnp.bfloat16)
        update = jnp.einsum(
            "rvi,vmij->rmj", value_rows, out_grid, preferred_element_type=jnp.float32
        ).reshape(all_rows, model_width)
        result = (hidden.astype(jnp.float32) + update).astype(jnp.bfloat16)
        return (value_rows.reshape(all_rows, value_width), result)

    def skip_forward(operands):
        return (operands[1], operands[2])

    def backward_layer(operands):
        grad_rows, old_input = operands
        grad_blocked = grad_rows.reshape(all_rows, model_blocks, tile_width)
        grad_values = jnp.einsum(
            "rmj,vmij->rvi", grad_blocked, out_grid, preferred_element_type=jnp.float32
        ).astype(jnp.bfloat16)
        extra_term = jnp.einsum(
            "rvj,bvij->rbi", grad_values, value_grid, preferred_element_type=jnp.float32
        ).reshape(all_rows, model_width)
        return (grad_rows.astype(jnp.float32) + extra_term).astype(jnp.bfloat16)

    def skip_backward(operands):
        return operands[1]

    first_input = activations_in.reshape(all_rows, model_width)
    value_store = jnp.zeros((all_rows, value_width), jnp.bfloat16)
    act_store = jnp.zeros((all_rows, model_width), jnp.bfloat16)
    carried = jnp.zeros((all_rows, model_width), jnp.bfloat16)
    for step_number in range(section_count):
        active = section_index == step_number
        hidden = jnp.where(section_index == 0, first_input, carried)
        value_store, act_store = lax.cond(
            active, forward_layer, skip_forward, (hidden, value_store, act_store)
        )
        if step_number + 1 < section_count:
            carried = from_behind(act_store, "section", 1)
    last_grad = cotangent.reshape(all_rows, model_width)
    grad_store = jnp.where(section_index == section_count - 1, last_grad, jnp.zeros_like(last_grad))
    input_store = jnp.zeros((all_rows, model_width), jnp.bfloat16)
    carried_grad = jnp.zeros((all_rows, model_width), jnp.bfloat16)
    for step_number in range(section_count):
        active = section_index == section_count - 1 - step_number
        if step_number > 0:
            grad_store = jnp.where(active, carried_grad, grad_store)
        input_store = lax.cond(active, backward_layer, skip_backward, (grad_store, input_store))
        if step_number + 1 < section_count:
            carried_grad = from_behind(input_store, "section", -1)
    grad_scale = 1.0 / math.sqrt(micro_count * tok_rows * shard_count)
    value_blocked = value_store.reshape(all_rows, value_blocks, tile_width)
    grad_blocked = grad_store.reshape(all_rows, model_blocks, tile_width)
    value_part = jnp.take(value_blocked, out_slot // model_blocks, axis=1)
    grad_part = jnp.take(grad_blocked, out_slot % model_blocks, axis=1)
    summed = lax.psum_scatter(
        jnp.einsum("rkc,rkd->kcd", value_part, grad_part, preferred_element_type=jnp.float32),
        "dp",
        scatter_dimension=0,
        tiled=True,
    )
    scaled = summed * grad_scale
    out_grad = jnp.where(own_live[:, None, None], scaled, jnp.zeros_like(scaled))
    section_out = act_store.reshape(micro_count, tok_rows, model_width)
    grad_out = input_store.reshape(micro_count, tok_rows, model_width)
    return (section_out[None], grad_out[None], out_grad[None])


def solution(mesh):
    in_specs = (
        P(None, "dp", None),
        P(None, "dp", None),
        P("section", None, None, None),
        P("section", None),
        P("section", "dp", None, None),
        P("section", None),
        P("section", None),
    )
    out_specs = (
        P("section", None, "dp", None),
        P("section", None, "dp", None),
        P("section", "dp", None, None),
    )
    return jax.shard_map(
        on_device, mesh=mesh, in_specs=in_specs, out_specs=out_specs, check_vma=False
    )
```

profile of v0, /device:TPU:2, one launch (start us, length us, event | category | flops | bytes accessed | tf_op | source)
XLA Modules:
  0.0 639.2 jit_solution(5982883603321064038)
XLA Ops:
  9.5 5.4 broadcast.209.clone
  14.9 19.4 %scatter_fusion = bf16[256,128,128]{2,1,0:T(8,128)(2,1)} fusion(bf16[256,128,128]{2,1,0:T(8,128)(2,1)} %broadcast.209.clone, s32[128]{0:T(128)S(1)} %fusion.38, bf16[128,128,128]{2,1,0:T(8,128)(2,1)} %bitcast.307), kind=kCustom, calls=%fused_computation.2 | custom fusion | bytes 12583424 | tf_op jit(solution)/shard_map/scatter | solution.py:19
  34.5 78.6 %all-gather.3.cloned.1.call-done = bf16[1,192,128,128]{3,2,0,1:T(8,128)(2,1)} async-done(((bf16[1,3,128,128]{3,2,0,1:T(8,128)(2,1)}), bf16[1,192,128,128]{3,2,0,1:T(8,128)(2,1)}) %all-gather.3.cloned.1.call-update) | async-done | bytes 6291472 | tf_op jit(solution)/shard_map/all_gather | solution.py:42
  113.1 5.9 bitcast_select_fusion
  119.0 5.3 broadcast.209.clone.1
  124.3 28.7 %scatter_fusion.1 = bf16[256,128,128]{2,1,0:T(8,128)(2,1)} fusion(bf16[256,128,128]{2,1,0:T(8,128)(2,1)} %broadcast.209.clone.1, s32[192]{0:T(256)S(1)} %bitcast.312, bf16[192,128,128]{2,1,0:T(8,128)(2,1)} %bitcast_select_fusion), kind=kCustom, calls=%fused_computation.3 | custom fusion | bytes 18875136 | tf_op jit(solution)/shard_map/scatter | solution.py:19
  154.7 4.2 copy.131
  161.8 18.7 %conditional.8 = (bf16[128,512]{0,1:T(8,128)(2,1)}, bf16[128,8192]{0,1:T(8,128)(2,1)}) conditional(s32[]{:T(128)} %convert_element_type.91, () %tuple.76, (bf16[128,8192]{1,0:T(8,128)(2,1)}, bf16[64,4,128,128]{3,2,1,0:T(8,128)(2,1)}, bf16[4,64,128,128]{3,2,1,0:T(8,128)(2,1)}) %tuple.158), branch_computations={%region_2.3_spmd, %region_3.4_spmd} | conditional | flops 2150694912 | bytes 77856840 | solution.py:83
  162.0 4.1 copy.115
  166.1 8.2 %fusion.1 = bf16[128,4,128]{0,2,1:T(8,128)(2,1)} fusion(bf16[128,64,128,1]{0,2,3,1:T(8,128)(2,1)} %bitcast.306, bf16[64,4,128,128]{3,2,1,0:T(8,128)(2,1)} %get-tuple-element.207), kind=kOutput, calls=%fused_computation.7 | convolution fusion | flops 1073807360 | bytes 10616832 | tf_op jit(solution)/shard_map/cond/branch_1_fun/rbi,bvij->rvj/dot_general | solution.py:50
  174.3 4.4 fusion.2
  180.5 4.1 copy.118
  190.3 4.1 copy.133
  197.8 4.1 copy.122
  201.9 25.1 %collective-permute-start.1 = (bf16[128,8192]{1,0:T(8,128)(2,1)}, bf16[128,8192]{1,0:T(8,128)(2,1)}, u32[]{:S(2)}, u32[]{:S(2)}) collective-permute-start(bf16[128,8192]{1,0:T(8,128)(2,1)} %copy.122), channel_id=1, source_target_pairs={{0,64},{64,128},{128,192},{1,65},{65,129},{129,193},{2,66},{66,130... | collective-permute-start | bytes 6291464 | tf_op jit(solution)/shard_map/ppermute | solution.py:13
  227.0 3.1 broadcast_select_fusion.1
  230.1 4.2 conditional.14
  230.1 4.1 copy.191
  235.7 29.9 %collective-permute-done.5 = bf16[128,8192]{1,0:T(8,128)(2,1)S(1)} collective-permute-done((bf16[128,8192]{1,0:T(8,128)(2,1)}, bf16[128,8192]{1,0:T(8,128)(2,1)S(1)}, u32[]{:S(2)}, u32[]{:S(2)}) %collective-permute-start.5) | collective-permute-done | bytes 2097184 | tf_op jit(solution)/shard_map/ppermute | solution.py:13
  268.4 27.1 %collective-permute-start.2 = (bf16[128,8192]{0,1:T(8,128)(2,1)}, bf16[128,8192]{0,1:T(8,128)(2,1)}, u32[]{:S(2)}, u32[]{:S(2)}) collective-permute-start(bf16[128,8192]{0,1:T(8,128)(2,1)} %get-tuple-element.131), channel_id=1, source_target_pairs={{0,64},{64,128},{128,192},{1,65},{65,129},{129,193},{2,66},{66,130... | collective-permute-start | bytes 6291464 | tf_op jit(solution)/shard_map/ppermute | solution.py:13
  295.6 4.1 copy.137
  299.6 4.1 copy.138
  303.7 9.6 %gather_fusion.1 = bf16[192,128,128]{2,1,0:T(8,128)(2,1)} fusion(bf16[128,64,128]{2,0,1:T(8,128)(2,1)} %copy.138, s32[1024]{0:T(1024)S(1)} %pad_clamp_fusion), kind=kCustom, calls=%fused_computation.1 | custom fusion | bytes 12583680 | tf_op jit(solution)/shard_map/jit(_take)/gather | solution.py:103
  315.2 8.8 %gather_fusion = bf16[192,128,128]{2,1,0:T(8,128)(2,1)} fusion(bf16[128,4,128]{2,0,1:T(8,128)(2,1)} %get-tuple-element.133, s32[1024]{0:T(1024)S(1)} %pad_clamp_fusion.1), kind=kCustom, calls=%fused_computation | custom fusion | bytes 12583680 | tf_op jit(solution)/shard_map/jit(_take)/gather | solution.py:102
  324.0 11.8 %fusion.30 = f32[192,128,128]{2,1,0:T(8,128)} fusion(bf16[192,128,128]{2,1,0:T(8,128)(2,1)} %gather_fusion.1, bf16[192,128,128]{2,1,0:T(8,128)(2,1)} %gather_fusion, pred[192]{0:T(512)(128)(4,1)S(1)} %get-tuple-element.233, pred[192]{0:T(512)(128)(4,1)S(1)} %get-tuple-element.232), kind=kOutput, calls=%fused_computation.51 | convolution fusion | flops 811597824 | bytes 25166208 | tf_op jit(solution)/shard_map/rkc,rkd->kcd/dot_general | solution.py:105
  337.3 20.5 %conditional.15 = (bf16[1,2,64,8192]{3,2,1,0:T(8,128)(2,1)}) conditional(s32[]{:T(128)} %convert_element_type.91, bf16[128,8192]{1,0:T(8,128)(2,1)} %get-tuple-element.229, (bf16[128,8192]{1,0:T(8,128)(2,1)S(1)}, bf16[4,64,128,128]{3,2,1,0:T(8,128)(2,1)}, bf16[64,4,128,128]{3,2,1,0:T(8,128)(2,1)}) %tuple.167), branch_computations={%region_16.17_spmd, %region_17.18_spmd} | conditional | flops 2150694912 | bytes 73662504 | solution.py:96
  337.6 6.4 fusion.29
  344.0 4.3 fusion.43
  348.3 5.6 copy.113
  354.0 3.9 add_convert_fusion
  357.9 4.1 copy.129
  362.0 268.2 %reduce-scatter.2.cloned.1.call-done = f32[3,128,128]{2,1,0:T(8,128)} async-done(((f32[192,128,128]{2,1,0:T(8,128)}), f32[3,128,128]{2,1,0:T(8,128)}) %reduce-scatter.2.cloned.1.call-update) | async-done | bytes 196624 | tf_op jit(solution)/shard_map/reduce_scatter | solution.py:104
  (50 shorter events, 30.3 us)
Async XLA Ops:
  7.2 105.9 %all-gather.3.cloned.1.call-start = ((), (), s32[]{:S(2)}) async-start(), calls=%async_computation.2 | async-start | bytes 6389760 | tf_op jit(solution)/shard_map/all_gather | solution.py:42
  7.9 622.3 %reduce-scatter.2.cloned.1.call-start = ((), (), s32[]{:S(2)}) async-start(), calls=%async_computation.1 | async-start | bytes 12779520 | tf_op jit(solution)/shard_map/reduce_scatter | solution.py:104
  14.9 19.4 %copy-start.16 = (s32[1,192]{1,0:T(1,128)S(1)}, s32[1,192]{1,0:T(1,128)}, u32[]{:S(2)}) copy-start(s32[1,192]{1,0:T(1,128)} %param.28) | copy-start | bytes 2308
  34.4 118.6 %copy-start.8 = (bf16[2,64,8192]{2,1,0:T(8,128)(2,1)}, bf16[2,64,8192]{2,1,0:T(8,128)(2,1)S(1)}, u32[]{:S(2)}) copy-start(bf16[2,64,8192]{2,1,0:T(8,128)(2,1)S(1)} %broadcast_select_fusion.3) | copy-start | bytes 6291460
  154.7 5.5 copy-start.7
  158.9 28.3 %collective-permute-start.3 = (bf16[128,8192]{1,0:T(8,128)(2,1)}, bf16[128,8192]{1,0:T(8,128)(2,1)}, u32[]{:S(2)}, u32[]{:S(2)}) collective-permute-start(bf16[128,8192]{1,0:T(8,128)(2,1)} %copy.131), channel_id=1, source_target_pairs={{64,0},{128,64},{192,128},{65,1},{129,65},{193,129},{66,2},{130,66... | collective-permute-start | bytes 6291464 | tf_op jit(solution)/shard_map/ppermute | solution.py:13
  166.1 8.2 %copy-start.4 = (bf16[4,64,128,128]{3,2,1,0:T(8,128)(2,1)S(1)}, bf16[4,64,128,128]{3,2,1,0:T(8,128)(2,1)}, u32[]{:S(2)}) copy-start(bf16[4,64,128,128]{3,2,1,0:T(8,128)(2,1)} %get-tuple-element.208) | copy-start | bytes 25165828 | tf_op jit(solution)/shard_map/cond
  174.3 4.4 copy-start.15
  184.5 11.2 %collective-permute-start = (bf16[128,8192]{1,0:T(8,128)(2,1)}, bf16[128,8192]{1,0:T(8,128)(2,1)}, u32[]{:S(2)}, u32[]{:S(2)}) collective-permute-start(bf16[128,8192]{1,0:T(8,128)(2,1)} %copy.118), channel_id=1, source_target_pairs={{0,64},{64,128},{128,192},{1,65},{65,129},{129,193},{2,66},{66,130... | collective-permute-start | bytes 6291464 | tf_op jit(solution)/shard_map/ppermute | solution.py:13
  194.4 32.6 %collective-permute-start.4 = (bf16[128,8192]{1,0:T(8,128)(2,1)}, bf16[128,8192]{1,0:T(8,128)(2,1)}, u32[]{:S(2)}, u32[]{:S(2)}) collective-permute-start(bf16[128,8192]{1,0:T(8,128)(2,1)} %copy.133), channel_id=1, source_target_pairs={{64,0},{128,64},{192,128},{65,1},{129,65},{193,129},{66,2},{130,66... | collective-permute-start | bytes 6291464 | tf_op jit(solution)/shard_map/ppermute | solution.py:13
  201.9 33.8 %collective-permute-start.1 = (bf16[128,8192]{1,0:T(8,128)(2,1)}, bf16[128,8192]{1,0:T(8,128)(2,1)}, u32[]{:S(2)}, u32[]{:S(2)}) collective-permute-start(bf16[128,8192]{1,0:T(8,128)(2,1)} %copy.122), channel_id=1, source_target_pairs={{0,64},{64,128},{128,192},{1,65},{65,129},{129,193},{2,66},{66,130... | collective-permute-start | bytes 6291464 | tf_op jit(solution)/shard_map/ppermute | solution.py:13
  234.4 31.2 %collective-permute-start.5 = (bf16[128,8192]{1,0:T(8,128)(2,1)}, bf16[128,8192]{1,0:T(8,128)(2,1)S(1)}, u32[]{:S(2)}, u32[]{:S(2)}) collective-permute-start(bf16[128,8192]{1,0:T(8,128)(2,1)} %get-tuple-element.229), channel_id=1, source_target_pairs={{64,0},{128,64},{192,128},{65,1},{129,65},{193,129},{66,2},{130,66... | collective-permute-start | bytes 6291464 | tf_op jit(solution)/shard_map/ppermute | solution.py:13
  268.4 44.9 %collective-permute-start.2 = (bf16[128,8192]{0,1:T(8,128)(2,1)}, bf16[128,8192]{0,1:T(8,128)(2,1)}, u32[]{:S(2)}, u32[]{:S(2)}) collective-permute-start(bf16[128,8192]{0,1:T(8,128)(2,1)} %get-tuple-element.131), channel_id=1, source_target_pairs={{0,64},{64,128},{128,192},{1,65},{65,129},{129,193},{2,66},{66,130... | collective-permute-start | bytes 6291464 | tf_op jit(solution)/shard_map/ppermute | solution.py:13
  335.7 1.6 copy-start.9
  337.6 6.4 copy-start.3
Sparse Core Ops, SparseCore 0:
  11.2 101.7 all-gather.2
  335.9 294.2 reduce-scatter.1
where the time goes:
time: 648 us; the launch traced here: 639 us
  waiting for transfers between devices  377 us (58%)
  local copies, waits for them, and re-layouts  125 us (19%)
  starting transfers between devices  58.8 us (9%)
  matrix products  35 us (5%)
  other arithmetic  27 us (4%)
  between operations  14.7 us (2%)
    reduce_scatter x1, waiting for transfers between devices, on_device(): lax.psum_scatter(jnp.einsum('rkc,rkd->kcd', value_part, grad_part, prefer...  268 us
    all_gather x1, waiting for transfers between devices, on_device(): gathered = lax.all_gather(out_tiles[0], 'dp', axis=0, tiled=True)  78.6 us
    ppermute x6, starting transfers between devices, from_behind(): lax.ppermute(value, axis, [(source, source + steps) for source in range(f...  58.7 us
    scatter x2, local copies, waits for them, and re-layouts, build_blocks(): grid = grid.at[tile_ids].set(tile_data)  48.1 us
    ppermute x6, waiting for transfers between devices, from_behind(): lax.ppermute(value, axis, [(source, source + steps) for source in range(f...  29.9 us
    another operation x5, local copies, waits for them, and re-layouts  18.1 us
  transfers between devices with their start and end apart: 8, of which 3 were waited for; matrix products, arithmetic and copies ran while one was open for 18% of the time, Pallas kernels for 0%

commit v1 on v0

--- a/solution.py
+++ b/solution.py
@@ -39,7 +39,15 @@
         -1
     )
     own_live = lax.dynamic_slice_in_dim(live_mask, shard_index * slot_share, slot_share)
-    gathered = lax.all_gather(out_tiles[0], "dp", axis=0, tiled=True)
+    gathered = jnp.concatenate(
+        lax.all_to_all(
+            jnp.stack(lax.axis_size("dp") * [out_tiles[0]], axis=0),
+            concat_axis=0,
+            axis_name="dp",
+            split_axis=0,
+        ),
+        0,
+    )
     masked_tiles = jnp.where(live_mask[:, None, None], gathered, jnp.zeros_like(gathered))
     value_grid = build_blocks(value_tiles[0], value_ids[0], model_blocks, value_blocks)
     out_grid = build_blocks(masked_tiles, out_slot, value_blocks, model_blocks)

time: 648 us -> 701 us (1.082)
  waiting for transfers between devices: 377 us -> 411 us
  starting transfers between devices: 58.8 us -> 72.9 us
    all_to_all x0 -> x1, waiting for transfers between devices: none -> 117 us  [on_device(): lax.all_to_all(jnp.stack(lax.axis_size('dp') * [out_tiles[0]], axis=0), c...]
    all_gather x1 -> x0, waiting for transfers between devices: 78.6 us -> none  [on_device(): gathered = lax.all_gather(out_tiles[0], 'dp', axis=0, tiled=True)]
    all_to_all x0 -> x1, starting transfers between devices: none -> 14.9 us  [on_device(): lax.all_to_all(jnp.stack(lax.axis_size('dp') * [out_tiles[0]], axis=0), c...]
    another operation x5 -> x6, local copies, waits for them, and re-layouts: 18.1 us -> 23.3 us
  transfers between devices with their start and end apart: 8 -> 8, of which waited for: 3 -> 3; matrix products, arithmetic and copies ran while one was open for 18% -> 16% of each run, Pallas kernels for 0% -> 0%
where the time goes in v1:
time: 701 us; the launch traced here: 691 us
  waiting for transfers between devices  411 us (59%)
  local copies, waits for them, and re-layouts  130 us (19%)
  starting transfers between devices  72.9 us (10%)
  matrix products  35.1 us (5%)
  other arithmetic  25.7 us (4%)
  between operations  14.7 us (2%)
    reduce_scatter x1, waiting for transfers between devices, on_device(): lax.psum_scatter(jnp.einsum('rkc,rkd->kcd', value_part, grad_part, prefer...  266 us
    all_to_all x1, waiting for transfers between devices, on_device(): lax.all_to_all(jnp.stack(lax.axis_size('dp') * [out_tiles[0]], axis=0), c...  117 us
    ppermute x6, starting transfers between devices, from_behind(): lax.ppermute(value, axis, [(source, source + steps) for source in range(f...  57.9 us
    scatter x2, local copies, waits for them, and re-layouts, build_blocks(): grid = grid.at[tile_ids].set(tile_data)  48.7 us
    ppermute x6, waiting for transfers between devices, from_behind(): lax.ppermute(value, axis, [(source, source + steps) for source in range(f...  27.5 us
    another operation x5, local copies, waits for them, and re-layouts  18.1 us
    all_to_all x1, starting transfers between devices, on_device(): lax.all_to_all(jnp.stack(lax.axis_size('dp') * [out_tiles[0]], axis=0), c...  14.9 us
  transfers between devices with their start and end apart: 8, of which 3 were waited for; matrix products, arithmetic and copies ran while one was open for 16% of the time, Pallas kernels for 0%

profile of v1, /device:TPU:2, one launch (start us, length us, event | category | flops | bytes accessed | tf_op | source)
XLA Modules:
  0.0 690.8 jit_solution(8522582110993664583)
XLA Ops:
  7.2 5.2 stack.3
  12.3 14.9 %all-to-all-start = ((bf16[64,3,128,128]{3,2,1,0:T(8,128)(2,1)}), bf16[64,3,128,128]{3,2,1,0:T(8,128)(2,1)}, u32[]{:S(2)}, u32[]{:S(2)}) async-start(bf16[64,3,128,128]{3,2,1,0:T(8,128)(2,1)} %stack.3), calls=%async_computation | async-start | bytes 12582912 | tf_op jit(solution)/shard_map/all_to_all | solution.py:43
  27.6 5.4 broadcast.210.clone
  33.0 19.5 %scatter_fusion = bf16[256,128,128]{2,1,0:T(8,128)(2,1)} fusion(bf16[256,128,128]{2,1,0:T(8,128)(2,1)} %broadcast.210.clone, s32[128]{0:T(128)S(1)} %fusion.38, bf16[128,128,128]{2,1,0:T(8,128)(2,1)} %bitcast.307), kind=kCustom, calls=%fused_computation.2 | custom fusion | bytes 12583424 | tf_op jit(solution)/shard_map/scatter | solution.py:19
  52.7 117.0 %all-to-all-done = bf16[64,3,128,128]{3,2,1,0:T(8,128)(2,1)} async-done(((bf16[64,3,128,128]{3,2,1,0:T(8,128)(2,1)}), bf16[64,3,128,128]{3,2,1,0:T(8,128)(2,1)}, u32[]{:S(2)}, u32[]{:S(2)}) %all-to-all-start) | async-done | bytes 6291488 | tf_op jit(solution)/shard_map/all_to_all | solution.py:43
  169.8 6.0 bitcast_select_fusion
  175.8 5.3 broadcast.210.clone.1
  181.1 29.1 %scatter_fusion.1 = bf16[256,128,128]{2,1,0:T(8,128)(2,1)} fusion(bf16[256,128,128]{2,1,0:T(8,128)(2,1)} %broadcast.210.clone.1, s32[192]{0:T(256)S(1)} %bitcast.312, bf16[192,128,128]{2,1,0:T(8,128)(2,1)} %bitcast_select_fusion), kind=kCustom, calls=%fused_computation.3 | custom fusion | bytes 18875136 | tf_op jit(solution)/shard_map/scatter | solution.py:19
  211.8 4.2 copy.92
  218.9 18.7 %conditional.8 = (bf16[128,512]{0,1:T(8,128)(2,1)}, bf16[128,8192]{0,1:T(8,128)(2,1)}) conditional(s32[]{:T(128)} %convert_element_type.91, () %tuple.76, (bf16[128,8192]{1,0:T(8,128)(2,1)}, bf16[64,4,128,128]{3,2,1,0:T(8,128)(2,1)}, bf16[4,64,128,128]{3,2,1,0:T(8,128)(2,1)}) %tuple.148), branch_computations={%region_2.3_spmd, %region_3.4_spmd} | conditional | flops 2150694912 | bytes 77856840 | solution.py:91
  219.1 4.1 copy.76
  223.2 8.2 %fusion.1 = bf16[128,4,128]{0,2,1:T(8,128)(2,1)} fusion(bf16[128,64,128,1]{0,2,3,1:T(8,128)(2,1)} %bitcast.306, bf16[64,4,128,128]{3,2,1,0:T(8,128)(2,1)} %get-tuple-element.182), kind=kOutput, calls=%fused_computation.7 | convolution fusion | flops 1073807360 | bytes 10616832 | tf_op jit(solution)/shard_map/cond/branch_1_fun/rbi,bvij->rvj/dot_general | solution.py:58
  231.4 4.4 fusion.2
  237.6 4.1 copy.79
  247.4 4.1 copy.94
  254.9 4.1 copy.83
  259.0 24.3 %collective-permute-start.1 = (bf16[128,8192]{1,0:T(8,128)(2,1)}, bf16[128,8192]{1,0:T(8,128)(2,1)}, u32[]{:S(2)}, u32[]{:S(2)}) collective-permute-start(bf16[128,8192]{1,0:T(8,128)(2,1)} %copy.83), channel_id=1, source_target_pairs={{0,64},{64,128},{128,192},{1,65},{65,129},{129,193},{2,66},{66,130... | collective-permute-start | bytes 6291464 | tf_op jit(solution)/shard_map/ppermute | solution.py:13
  286.4 4.2 conditional.14
  286.4 4.1 copy.152
  292.0 27.5 %collective-permute-done.5 = bf16[128,8192]{1,0:T(8,128)(2,1)S(1)} collective-permute-done((bf16[128,8192]{1,0:T(8,128)(2,1)}, bf16[128,8192]{1,0:T(8,128)(2,1)S(1)}, u32[]{:S(2)}, u32[]{:S(2)}) %collective-permute-start.5) | collective-permute-done | bytes 2097184 | tf_op jit(solution)/shard_map/ppermute | solution.py:13
  322.2 27.1 %collective-permute-start.2 = (bf16[128,8192]{0,1:T(8,128)(2,1)}, bf16[128,8192]{0,1:T(8,128)(2,1)}, u32[]{:S(2)}, u32[]{:S(2)}) collective-permute-start(bf16[128,8192]{0,1:T(8,128)(2,1)} %get-tuple-element.131), channel_id=1, source_target_pairs={{0,64},{64,128},{128,192},{1,65},{65,129},{129,193},{2,66},{66,130... | collective-permute-start | bytes 6291464 | tf_op jit(solution)/shard_map/ppermute | solution.py:13
  349.4 4.1 copy.98
  353.5 4.1 copy.99
  357.6 9.6 %gather_fusion.1 = bf16[192,128,128]{2,1,0:T(8,128)(2,1)} fusion(bf16[128,64,128]{2,0,1:T(8,128)(2,1)} %copy.99, s32[1024]{0:T(1024)S(1)} %pad_clamp_fusion), kind=kCustom, calls=%fused_computation.1 | custom fusion | bytes 12583680 | tf_op jit(solution)/shard_map/jit(_take)/gather | solution.py:111
  369.1 8.8 %gather_fusion = bf16[192,128,128]{2,1,0:T(8,128)(2,1)} fusion(bf16[128,4,128]{2,0,1:T(8,128)(2,1)} %get-tuple-element.133, s32[1024]{0:T(1024)S(1)} %pad_clamp_fusion.1), kind=kCustom, calls=%fused_computation | custom fusion | bytes 12583680 | tf_op jit(solution)/shard_map/jit(_take)/gather | solution.py:110
  377.9 11.8 %fusion.30 = f32[192,128,128]{2,1,0:T(8,128)} fusion(bf16[192,128,128]{2,1,0:T(8,128)(2,1)} %gather_fusion.1, bf16[192,128,128]{2,1,0:T(8,128)(2,1)} %gather_fusion, pred[192]{0:T(512)(128)(4,1)S(1)} %get-tuple-element.208, pred[192]{0:T(512)(128)(4,1)S(1)} %get-tuple-element.207), kind=kOutput, calls=%fused_computation.51 | convolution fusion | flops 811597824 | bytes 25166208 | tf_op jit(solution)/shard_map/rkc,rkd->kcd/dot_general | solution.py:113
  391.2 20.5 %conditional.15 = (bf16[1,2,64,8192]{3,2,1,0:T(8,128)(2,1)}) conditional(s32[]{:T(128)} %convert_element_type.91, bf16[128,8192]{1,0:T(8,128)(2,1)} %get-tuple-element.204, (bf16[128,8192]{1,0:T(8,128)(2,1)S(1)}, bf16[4,64,128,128]{3,2,1,0:T(8,128)(2,1)}, bf16[64,4,128,128]{3,2,1,0:T(8,128)(2,1)}) %tuple.157), branch_computations={%region_16.17_spmd, %region_17.18_spmd} | conditional | flops 2150694912 | bytes 73662504 | solution.py:104
  391.5 6.4 fusion.29
  397.9 4.3 fusion.43
  402.2 5.6 copy.75
  411.7 4.1 copy.90
  415.8 266.0 %reduce-scatter.2.cloned.1.call-done = f32[3,128,128]{2,1,0:T(8,128)} async-done(((f32[192,128,128]{2,1,0:T(8,128)}), f32[3,128,128]{2,1,0:T(8,128)}) %reduce-scatter.2.cloned.1.call-update) | async-done | bytes 196624 | tf_op jit(solution)/shard_map/reduce_scatter | solution.py:112
  (54 shorter events, 35.4 us)
Async XLA Ops:
  12.3 15.0 %copy-start.17 = (s32[1,64]{1,0:T(1,128)S(1)}, s32[1,64]{1,0:T(1,128)}, u32[]{:S(2)}) copy-start(s32[1,64]{1,0:T(1,128)} %param.29) | copy-start | bytes 772
  12.3 15.3 %copy-start.18 = (s32[1,128]{1,0:T(1,128)S(1)}, s32[1,128]{1,0:T(1,128)}, u32[]{:S(2)}) copy-start(s32[1,128]{1,0:T(1,128)} %param.26) | copy-start | bytes 1540
  12.3 157.5 %all-to-all-start = ((bf16[64,3,128,128]{3,2,1,0:T(8,128)(2,1)}), bf16[64,3,128,128]{3,2,1,0:T(8,128)(2,1)}, u32[]{:S(2)}, u32[]{:S(2)}) async-start(bf16[64,3,128,128]{3,2,1,0:T(8,128)(2,1)} %stack.3), calls=%async_computation | async-start | bytes 12582912 | tf_op jit(solution)/shard_map/all_to_all | solution.py:43
  27.3 654.5 %reduce-scatter.2.cloned.1.call-start = ((), (), s32[]{:S(2)}) async-start(), calls=%async_computation.2 | async-start | bytes 12779520 | tf_op jit(solution)/shard_map/reduce_scatter | solution.py:112
  33.0 19.5 %copy-start.16 = (s32[1,192]{1,0:T(1,128)S(1)}, s32[1,192]{1,0:T(1,128)}, u32[]{:S(2)}) copy-start(s32[1,192]{1,0:T(1,128)} %param.28) | copy-start | bytes 2308
  52.7 157.5 %copy-start.8 = (bf16[2,64,8192]{2,1,0:T(8,128)(2,1)}, bf16[2,64,8192]{2,1,0:T(8,128)(2,1)S(1)}, u32[]{:S(2)}) copy-start(bf16[2,64,8192]{2,1,0:T(8,128)(2,1)S(1)} %broadcast_select_fusion.3) | copy-start | bytes 6291460
  211.8 5.5 copy-start.7
  216.0 28.3 %collective-permute-start.3 = (bf16[128,8192]{1,0:T(8,128)(2,1)}, bf16[128,8192]{1,0:T(8,128)(2,1)}, u32[]{:S(2)}, u32[]{:S(2)}) collective-permute-start(bf16[128,8192]{1,0:T(8,128)(2,1)} %copy.92), channel_id=1, source_target_pairs={{64,0},{128,64},{192,128},{65,1},{129,65},{193,129},{66,2},{130,66... | collective-permute-start | bytes 6291464 | tf_op jit(solution)/shard_map/ppermute | solution.py:13
  223.2 8.2 %copy-start.4 = (bf16[4,64,128,128]{3,2,1,0:T(8,128)(2,1)S(1)}, bf16[4,64,128,128]{3,2,1,0:T(8,128)(2,1)}, u32[]{:S(2)}) copy-start(bf16[4,64,128,128]{3,2,1,0:T(8,128)(2,1)} %get-tuple-element.183) | copy-start | bytes 25165828 | tf_op jit(solution)/shard_map/cond
  231.4 4.4 copy-start.15
  241.7 11.2 %collective-permute-start = (bf16[128,8192]{1,0:T(8,128)(2,1)}, bf16[128,8192]{1,0:T(8,128)(2,1)}, u32[]{:S(2)}, u32[]{:S(2)}) collective-permute-start(bf16[128,8192]{1,0:T(8,128)(2,1)} %copy.79), channel_id=1, source_target_pairs={{0,64},{64,128},{128,192},{1,65},{65,129},{129,193},{2,66},{66,130... | collective-permute-start | bytes 6291464 | tf_op jit(solution)/shard_map/ppermute | solution.py:13
  251.5 31.8 %collective-permute-start.4 = (bf16[128,8192]{1,0:T(8,128)(2,1)}, bf16[128,8192]{1,0:T(8,128)(2,1)}, u32[]{:S(2)}, u32[]{:S(2)}) collective-permute-start(bf16[128,8192]{1,0:T(8,128)(2,1)} %copy.94), channel_id=1, source_target_pairs={{64,0},{128,64},{192,128},{65,1},{129,65},{193,129},{66,2},{130,66... | collective-permute-start | bytes 6291464 | tf_op jit(solution)/shard_map/ppermute | solution.py:13
  259.0 32.9 %collective-permute-start.1 = (bf16[128,8192]{1,0:T(8,128)(2,1)}, bf16[128,8192]{1,0:T(8,128)(2,1)}, u32[]{:S(2)}, u32[]{:S(2)}) collective-permute-start(bf16[128,8192]{1,0:T(8,128)(2,1)} %copy.83), channel_id=1, source_target_pairs={{0,64},{64,128},{128,192},{1,65},{65,129},{129,193},{2,66},{66,130... | collective-permute-start | bytes 6291464 | tf_op jit(solution)/shard_map/ppermute | solution.py:13
  290.7 28.8 %collective-permute-start.5 = (bf16[128,8192]{1,0:T(8,128)(2,1)}, bf16[128,8192]{1,0:T(8,128)(2,1)S(1)}, u32[]{:S(2)}, u32[]{:S(2)}) collective-permute-start(bf16[128,8192]{1,0:T(8,128)(2,1)} %get-tuple-element.204), channel_id=1, source_target_pairs={{64,0},{128,64},{192,128},{65,1},{129,65},{193,129},{66,2},{130,66... | collective-permute-start | bytes 6291464 | tf_op jit(solution)/shard_map/ppermute | solution.py:13
  322.2 44.9 %collective-permute-start.2 = (bf16[128,8192]{0,1:T(8,128)(2,1)}, bf16[128,8192]{0,1:T(8,128)(2,1)}, u32[]{:S(2)}, u32[]{:S(2)}) collective-permute-start(bf16[128,8192]{0,1:T(8,128)(2,1)} %get-tuple-element.131), channel_id=1, source_target_pairs={{0,64},{64,128},{128,192},{1,65},{65,129},{129,193},{2,66},{66,130... | collective-permute-start | bytes 6291464 | tf_op jit(solution)/shard_map/ppermute | solution.py:13
  389.6 1.6 copy-start.9
  391.5 6.4 copy-start.3
Sparse Core Ops, SparseCore 0:
  389.8 291.9 reduce-scatter.1
